TPU v7x, 512 devices: a whole 4x8x8 slice. The times are simulated.
512 devices in a mesh: col: 32 (over x_lo, z, core), rec: 16 (over x_hi, y).
Axes of the slice: x: 4 (x_hi: 2, x_lo: 2; x = x_hi * 2 + x_lo), y: 8, z: 8, core: 2. Of those that a mesh axis runs over, the one named last changes fastest.
Arguments:
- design: bfloat16 [4096, 16384], P('rec', 'col')
- record_weight: float32 [4096], P('rec'), may hold values from 0.5 to 3.47
Outputs:
- rotated_design: bfloat16 [4096, 16384], P('rec', 'col')
- column_rms: float32 [16384], P('col')
All inputs are finite; a program needn't handle non-finite values.
Results may differ from a plain program's by a relative error of at most 0.0088.
Values may be sent and summed in bfloat16 or wider, within the bound.
No kernel may reach another device: no remote copies, remote signals or barrier semaphores. Data moves between devices by JAX's collectives and lax.ppermute only.
A program may use at most 64 MiB of HBM per device.

v0:
```python
import jax
import jax.numpy as jnp
from jax import lax
from jax.sharding import PartitionSpec as P

ROUNDS = 3
SWEEPS = 6
eps_angle = 0.01


def from_behind(value, axis, steps):
    count = lax.axis_size(axis)
    leading, last = (max(0, -steps), min(count, count - steps))
    return lax.ppermute(value, axis, [(source, source + steps) for source in range(leading, last)])


def jacobi_sweeps(gram_matrix, width):
    top_left = gram_matrix[:width, :width]
    top_right = gram_matrix[:width, width:]
    low_left = gram_matrix[width:, :width]
    low_right = gram_matrix[width:, width:]
    identity = jnp.eye(2 * width, dtype=jnp.float32)
    rot_first = identity[:, :width]
    rot_second = identity[:, width:]
    for sweep_index in range(SWEEPS):
        if sweep_index > 0:
            top_right = jnp.roll(top_right, -1, axis=1)
            low_left = jnp.roll(low_left, -1, axis=0)
            low_right = jnp.roll(jnp.roll(low_right, -1, axis=0), -1, axis=1)
            rot_second = jnp.roll(rot_second, -1, axis=1)
        first_diag = jnp.diagonal(top_left)
        second_diag = jnp.diagonal(low_right)
        coupling = jnp.diagonal(top_right)
        spread = second_diag - first_diag
        tangent = (
            2.0
            * coupling
            * spread
            / (
                spread * spread
                + 4.0 * coupling * coupling
                + eps_angle * (first_diag + second_diag) ** 2
            )
        )
        half_angle = 0.5 * jnp.arctan(tangent)
        cosine = jnp.cos(half_angle)
        sine_value = jnp.sin(half_angle)
        cos_col = cosine[None, :]
        sin_col = sine_value[None, :]
        cos_row = cosine[:, None]
        sin_row = sine_value[:, None]
        left_a = top_left * cos_col - top_right * sin_col
        right_a = top_left * sin_col + top_right * cos_col
        left_b = low_left * cos_col - low_right * sin_col
        right_b = low_left * sin_col + low_right * cos_col
        top_left = cos_row * left_a - sin_row * left_b
        low_left = sin_row * left_a + cos_row * left_b
        top_right = cos_row * right_a - sin_row * right_b
        low_right = sin_row * right_a + cos_row * right_b
        rot_first, rot_second = (
            rot_first * cos_col - rot_second * sin_col,
            rot_first * sin_col + rot_second * cos_col,
        )
    rot_second = jnp.roll(rot_second, SWEEPS - 1, axis=1)
    return jnp.concatenate([rot_first, rot_second], axis=1)


def send_right(block):
    return from_behind(block, "col", 1)


def send_left(block):
    return from_behind(block, "col", -1)


def inner_products(left_part, right_part):
    return lax.dot_general(
        left_part, right_part, (((0,), (0,)), ((), ())), preferred_element_type=jnp.float32
    )


def local(design, record_weight):
    width = design.shape[1] // 2
    weighted = (design.astype(jnp.float32) * record_weight[:, None]).astype(jnp.bfloat16)
    upper_block = weighted[:, :width]
    lower_block = weighted[:, width:]
    position = lax.axis_index("col")
    device_count = lax.axis_size("col")
    for round_index in range(ROUNDS):
        moving = round_index + 1 < ROUNDS
        pair_data = jnp.concatenate([upper_block, lower_block], axis=1)
        gram_matrix = lax.psum(inner_products(pair_data, pair_data), "rec")
        rotation = jacobi_sweeps(gram_matrix, width).astype(jnp.bfloat16)
        rotated = jnp.dot(pair_data, rotation, preferred_element_type=jnp.float32).astype(
            jnp.bfloat16
        )
        new_upper = rotated[:, :width]
        new_lower = rotated[:, width:]
        if moving:
            from_right = send_left(new_lower)
            from_left = send_right(jnp.where(position == 0, new_lower, new_upper))
        if moving:
            upper_block = jnp.where(position == 0, new_upper, from_left)
            lower_block = jnp.where(position == device_count - 1, new_upper, from_right)
        else:
            upper_block = new_upper
            lower_block = new_lower
    rotated_design = jnp.concatenate([upper_block, lower_block], axis=1)
    squares = jnp.sum(jnp.square(rotated_design.astype(jnp.float32)), axis=0)
    totals = lax.psum(squares, "rec")
    record_total = design.shape[0] * lax.axis_size("rec")
    column_rms = jnp.sqrt(totals / record_total + 1e-06)
    return (rotated_design, column_rms)


def solution(mesh):
    placed = (P("rec", "col"), P("rec"))
    return jax.shard_map(
        local, mesh=mesh, in_specs=placed, out_specs=(P("rec", "col"), P("col")), check_vma=False
    )
```

profile of v0, /device:TPU:64, one launch (start us, length us, event | category | flops | bytes accessed | tf_op | source)
XLA Modules:
  0.0 738.1 jit_solution(11142493049382048583)
XLA Ops:
  7.2 2.5 fusion.33
  9.9 168.6 %all-reduce.4.cloned.1.call-done = f32[512,512]{1,0:T(8,128)} async-done(((f32[512,512]{1,0:T(8,128)}), f32[512,512]{1,0:T(8,128)}) %all-reduce.4.cloned.1.call-update) | async-done | bytes 1048592 | tf_op jit(solution)/shard_map/psum | solution.py:92
  179.6 2.3 gather_fusion
  182.0 2.3 gather_fusion.2
  184.3 2.3 gather_fusion.1
  187.3 2.3 gather_fusion.5
  189.9 2.3 gather_fusion.4
  192.3 2.3 gather_fusion.3
  195.2 2.3 gather_fusion.8
  203.3 2.3 gather_fusion.11
  211.3 2.3 gather_fusion.14
  216.4 2.5 gather_fusion.13
  223.2 2.9 gather_fusion.17
  236.0 3.6 collective-permute-start.1
  243.5 162.9 %all-reduce.6.cloned.1.call-done = f32[512,512]{1,0:T(8,128)} async-done(((f32[512,512]{1,0:T(8,128)}), f32[512,512]{1,0:T(8,128)}) %all-reduce.6.cloned.1.call-update) | async-done | bytes 1048592 | tf_op jit(solution)/shard_map/psum | solution.py:92
  415.3 2.3 gather_fusion.23
  423.3 2.3 gather_fusion.26
  431.4 2.3 gather_fusion.29
  439.5 2.3 gather_fusion.32
  444.5 2.6 gather_fusion.31
  452.1 2.9 gather_fusion.35
  456.1 2.9 gather_fusion.33
  459.3 2.9 gather_fusion.34
  466.6 3.6 collective-permute-start.3
  474.1 163.0 %all-reduce.8.cloned.1.call-done = f32[512,512]{1,0:T(8,128)} async-done(((f32[512,512]{1,0:T(8,128)}), f32[512,512]{1,0:T(8,128)}) %all-reduce.8.cloned.1.call-update) | async-done | bytes 1048592 | tf_op jit(solution)/shard_map/psum | solution.py:92
  646.0 2.3 gather_fusion.41
  654.0 2.3 gather_fusion.44
  662.1 2.3 gather_fusion.47
  670.1 2.3 gather_fusion.50
  675.2 2.6 gather_fusion.49
  680.7 2.3 gather_fusion.53
  689.8 40.8 %psum.31 = f32[512]{0:T(512)S(1)} all-reduce(f32[512]{0:T(512)S(1)} %get-tuple-element.130), channel_id=1, replica_groups=mesh['col'=32,'rec'=16] {'rec'}, use_global_device_ids=true, to_apply=%region_4.5 | all-reduce | flops 512 | bytes 4096 | tf_op jit(solution)/shard_map/psum | solution.py:110
  (308 shorter events, 115.1 us)
Async XLA Ops:
  7.2 171.3 %all-reduce.4.cloned.1.call-start = ((), (), s32[]{:S(2)}) async-start(), calls=%async_computation | async-start | bytes 2097152 | tf_op jit(solution)/shard_map/psum | solution.py:92
  9.7 396.8 %all-reduce.6.cloned.1.call-start = ((), (), s32[]{:S(2)}) async-start(), calls=%async_computation.1 | async-start | bytes 2097152 | tf_op jit(solution)/shard_map/psum | solution.py:92
  182.0 4.8 copy-start
  229.8 2.4 copy-start.8
  229.8 2.5 copy-start.3
  232.7 1.0 copy-start.7
  232.8 0.8 copy-start.10
  234.0 6.3 collective-permute-start
  236.0 6.1 collective-permute-start.1
  242.1 1.3 copy-start.5
  243.5 393.7 %all-reduce.8.cloned.1.call-start = ((), (), s32[]{:S(2)}) async-start(), calls=%async_computation.2 | async-start | bytes 2097152 | tf_op jit(solution)/shard_map/psum | solution.py:92
  410.0 4.8 copy-start.1
  459.3 3.0 copy-start.9
  459.3 3.8 copy-start.4
  463.4 0.9 copy-start.6
  464.7 6.3 collective-permute-start.2
  466.6 6.1 collective-permute-start.3
  640.6 4.8 copy-start.2
Sparse Core Ops, SparseCore 0:
  10.9 167.4 all-reduce.3
  243.6 162.8 all-reduce.5
  474.2 162.8 all-reduce.7
where the time goes:
time: 746 us; the launch traced here: 738 us
  waiting for transfers between devices  500 us (67%)
  local copies, waits for them, and re-layouts  145 us (19%)
  blocking collectives  40.8 us (5%)
  other arithmetic  18.2 us (2%)
  between operations  16.3 us (2%)
  starting transfers between devices  11.2 us (2%)
    psum x3, waiting for transfers between devices, local(): gram_matrix = lax.psum(inner_products(pair_data, pair_data), 'rec')  495 us
    gather x18, local copies, waits for them, and re-layouts, jacobi_sweeps(): second_diag = jnp.diagonal(low_right)  43.4 us
    gather x18, local copies, waits for them, and re-layouts, jacobi_sweeps(): first_diag = jnp.diagonal(top_left)  43.4 us
    gather x18, local copies, waits for them, and re-layouts, jacobi_sweeps(): coupling = jnp.diagonal(top_right)  42.8 us
    psum x1, blocking collectives, local(): totals = lax.psum(squares, 'rec')  40.8 us
  transfers between devices with their start and end apart: 7, of which 7 were waited for; matrix products, arithmetic and copies ran while one was open for 0% of the time, Pallas kernels for 0%

commit v1 on v0

--- a/solution.py
+++ b/solution.py
@@ -89,7 +89,13 @@
     for round_index in range(ROUNDS):
         moving = round_index + 1 < ROUNDS
         pair_data = jnp.concatenate([upper_block, lower_block], axis=1)
-        gram_matrix = lax.psum(inner_products(pair_data, pair_data), "rec")
+
+        def convert_things_on_mesh(panel, link_axis):
+            arr_out = lax.all_gather(panel, link_axis)
+            spare = jnp.sum(arr_out, axis=0)
+            return spare
+
+        gram_matrix = convert_things_on_mesh(inner_products(pair_data, pair_data), "rec")
         rotation = jacobi_sweeps(gram_matrix, width).astype(jnp.bfloat16)
         rotated = jnp.dot(pair_data, rotation, preferred_element_type=jnp.float32).astype(
             jnp.bfloat16

time: 746 us -> 963 us (1.29)
  the two profiles are of different devices: /device:TPU:64 before, /device:TPU:2 now
where the time goes in v1:
time: 963 us; the launch traced here: 960 us
  waiting for transfers between devices  694 us (72%)
  local copies, waits for them, and re-layouts  141 us (15%)
  other arithmetic  45.3 us (5%)
  blocking collectives  38.9 us (4%)
  between operations  16 us (2%)
  starting transfers between devices  15.5 us (2%)
    all_gather x3, waiting for transfers between devices, convert_things_on_mesh(): arr_out = lax.all_gather(panel, link_axis)  689 us
    gather x18, local copies, waits for them, and re-layouts, jacobi_sweeps(): coupling = jnp.diagonal(top_right)  44 us
    gather x18, local copies, waits for them, and re-layouts, jacobi_sweeps(): first_diag = jnp.diagonal(top_left)  44 us
    gather x18, local copies, waits for them, and re-layouts, jacobi_sweeps(): second_diag = jnp.diagonal(low_right)  42.8 us
    psum x1, blocking collectives, local(): totals = lax.psum(squares, 'rec')  38.9 us
    reduce_sum x3, other arithmetic, convert_things_on_mesh(): spare = jnp.sum(arr_out, axis=0)  23.9 us
  transfers between devices with their start and end apart: 7, of which 7 were waited for; matrix products, arithmetic and copies ran while one was open for 0% of the time, Pallas kernels for 0%

profile of v1, /device:TPU:2, one launch (start us, length us, event | category | flops | bytes accessed | tf_op | source)
XLA Modules:
  0.0 960.2 jit_solution(9625380921237258657)
XLA Ops:
  7.2 2.5 fusion.33
  9.9 235.2 %all-gather.7.cloned.1.call-done = f32[8192,512]{1,0:T(8,128)} async-done(((f32[512,512]{1,0:T(8,128)}), f32[8192,512]{1,0:T(8,128)}) %all-gather.7.cloned.1.call-update) | async-done | bytes 16777232 | tf_op jit(solution)/shard_map/all_gather | solution.py:94
  245.1 8.0 reduce_sum.36
  253.1 2.9 gather_fusion
  261.3 2.3 gather_fusion.5
  269.3 2.3 gather_fusion.8
  277.3 2.3 gather_fusion.11
  285.4 2.3 gather_fusion.14
  290.4 2.5 gather_fusion.13
  297.3 2.9 gather_fusion.17
  311.7 5.8 collective-permute-start.1
  321.4 227.0 %all-gather.9.cloned.1.call-done = f32[8192,512]{1,0:T(8,128)} async-done(((f32[512,512]{1,0:T(8,128)}), f32[8192,512]{1,0:T(8,128)}) %all-gather.9.cloned.1.call-update) | async-done | bytes 16777232 | tf_op jit(solution)/shard_map/all_gather | solution.py:94
  548.4 8.0 reduce_sum.37
  556.4 2.6 gather_fusion.18
  564.3 2.3 gather_fusion.23
  572.4 2.3 gather_fusion.26
  580.4 2.3 gather_fusion.29
  588.5 2.3 gather_fusion.32
  593.6 2.6 gather_fusion.31
  601.1 2.9 gather_fusion.35
  605.2 2.9 gather_fusion.33
  616.1 5.8 collective-permute-start.3
  625.7 227.1 %all-gather.11.cloned.1.call-done = f32[8192,512]{1,0:T(8,128)} async-done(((f32[512,512]{1,0:T(8,128)}), f32[8192,512]{1,0:T(8,128)}) %all-gather.11.cloned.1.call-update) | async-done | bytes 16777232 | tf_op jit(solution)/shard_map/all_gather | solution.py:94
  852.8 8.0 reduce_sum.38
  860.8 2.8 gather_fusion.36
  869.0 2.3 gather_fusion.41
  877.0 2.3 gather_fusion.44
  885.1 2.3 gather_fusion.47
  893.1 2.3 gather_fusion.50
  898.2 2.5 gather_fusion.49
  903.7 2.9 gather_fusion.53
  913.9 38.9 %psum.7 = f32[512]{0:T(512)S(1)} all-reduce(f32[512]{0:T(512)S(1)} %get-tuple-element.130), channel_id=1, replica_groups=mesh['col'=32,'rec'=16] {'rec'}, use_global_device_ids=true, to_apply=%region_4.5 | all-reduce | flops 512 | bytes 4096 | tf_op jit(solution)/shard_map/psum | solution.py:116
  (291 shorter events, 122.3 us)
Async XLA Ops:
  7.2 237.9 %all-gather.7.cloned.1.call-start = ((), (), s32[]{:S(2)}) async-start(), calls=%async_computation | async-start | bytes 17825792 | tf_op jit(solution)/shard_map/all_gather | solution.py:94
  9.7 538.7 %all-gather.9.cloned.1.call-start = ((), (), s32[]{:S(2)}) async-start(), calls=%async_computation.1 | async-start | bytes 17825792 | tf_op jit(solution)/shard_map/all_gather | solution.py:94
  309.8 8.4 collective-permute-start
  311.7 8.3 collective-permute-start.1
  320.0 228.4 %copy-start = (bf16[256,256]{1,0:T(8,128)(2,1)}, bf16[256,256]{1,0:T(8,128)(2,1)S(1)}, u32[]{:S(2)}) copy-start(bf16[256,256]{1,0:T(8,128)(2,1)S(1)} %get-tuple-element.127) | copy-start | bytes 393220
  321.3 531.5 %all-gather.11.cloned.1.call-start = ((), (), s32[]{:S(2)}) async-start(), calls=%async_computation.2 | async-start | bytes 17825792 | tf_op jit(solution)/shard_map/all_gather | solution.py:94
  614.2 8.4 collective-permute-start.2
  616.1 8.3 collective-permute-start.3
Sparse Core Ops, SparseCore 0:
  11.2 233.8 all-gather.6
  321.5 226.9 all-gather.8
  625.9 226.9 all-gather.10
